TPU v7x, 512 devices: a whole 4x4x16 slice. The times are simulated.
512 devices in a mesh: section: 2 (over core), dp: 64 (over z, x), mp: 4 (over y).
Axes of the slice: x: 4, y: 4, z: 16, core: 2. Of those that a mesh axis runs over, the one named last changes fastest.
Arguments:
- states: bfloat16 [512, 24, 4096], P('dp')
- norm_gain: float32 [4096], replicated, may hold values from 0.1 to 1.9
- key_weight: bfloat16 [4096, 4096], P('dp', ('section', 'mp')), may hold values from -0.09375 to 0.09375
- value_weight: bfloat16 [4096, 4096], P('dp', ('section', 'mp')), may hold values from -0.09375 to 0.09375
- pass_len: int32 [512], P('dp'), may hold values from 1 to 24
- retrieval: int32 [64, 64], replicated, may hold values from 0 to 511, as said below
- queries: bfloat16 [64, 32, 4096], P('dp', None, ('section', 'mp'))
Outputs:
- context: bfloat16 [64, 32, 4096], P('dp', None, ('section', 'mp'))
- passage_scores: float32 [64, 64], P('dp')
Inputs may be any that keep to these rules, and one draw needn't show every extreme that they name: `retrieval`: each question's list names 64 different passages. Counting passages of one block of 8 ids (the same id // 8), a list names passages of between 32 and 63 different blocks, at most 2 from any block, and exactly 2 from at least one. Popular passages recur in many lists.
All inputs are finite; a program needn't handle non-finite values.
Results may differ from a plain program's by a relative error of at most 0.013.
Values may be sent and summed in bfloat16 or wider, within the bound.
No kernel may reach another device: no remote copies, remote signals or barrier semaphores. Data moves between devices by JAX's collectives and lax.ppermute only.
A program may use at most 128 MiB of HBM per device.

v0:
```python
import jax
import jax.numpy as jnp
from jax import lax
from jax.sharding import PartitionSpec as P

HS = 64
WIRE = jnp.bfloat16


def _plane_shape(mesh):
    n_dp = mesh.shape["dp"]
    try:
        xs = {d.coords[0] for d in mesh.devices[0, :, 0]}
        nx = len(xs)
    except Exception:
        nx = 2 if n_dp % 2 == 0 else 1
    return (n_dp // nx, nx)


def _ring_perm(nz, nx, along, step):
    pairs = []
    for z in range(nz):
        for x in range(nx):
            if along == "x":
                dst = z * nx + (x + step) % nx
            else:
                dst = (z + step) % nz * nx + x
            pairs.append((z * nx + x, dst))
    return pairs


def _send(tree, perm):
    return jax.tree.map(lambda a: lax.ppermute(a, "dp", perm), tree)


def _gather_ring(block, n, fwd, bwd):
    if n == 1:
        return block[None]
    rel = [None] * n
    rel[0] = block
    f = block
    g = block
    for k in range(1, (n - 1) // 2 + 1):
        f = lax.ppermute(f, "dp", fwd)
        g = lax.ppermute(g, "dp", bwd)
        rel[n - k] = f
        rel[k] = g
    if n % 2 == 0:
        half = n // 2
        if block.shape[0] >= 2:
            cut = block.shape[0] // 2
            a = lax.ppermute(f[:cut], "dp", fwd)
            b = lax.ppermute(g[cut:], "dp", bwd)
            rel[half] = jnp.concatenate([a, b], axis=0)
        else:
            rel[half] = lax.ppermute(f, "dp", fwd)
    return jnp.stack(rel)


def _combine(a, b):
    ma, la, oa, ea = a
    mb, lb, ob, eb = b
    m = jnp.maximum(ma, mb)
    sa = jnp.where(ma == m, 1.0, jnp.exp(ma - m))
    sb = jnp.where(mb == m, 1.0, jnp.exp(mb - m))
    l = sa * la + sb * lb
    sa_o = jnp.swapaxes(sa, -1, -2)[..., None]
    sb_o = jnp.swapaxes(sb, -1, -2)[..., None]
    o = oa * sa_o + ob * sb_o
    e = ea * sa[..., None] + eb * sb[..., None]
    return (m, l, o, e)


def _to_wire(s):
    m, l, o, e = s
    return (m, l, o.astype(WIRE), e.astype(WIRE))


def _from_wire(s):
    m, l, o, e = s
    return (m, l, o.astype(jnp.float32), e.astype(jnp.float32))


def _reduce_ring(state, axis, me, n, fwd, bwd):

    def chunk(r):
        idx = (me + r) % n
        return jax.tree.map(lambda a: lax.dynamic_index_in_dim(a, idx, axis, keepdims=False), state)

    if n == 1:
        return chunk(0)
    nb = n // 2
    nf = n - 1 - nb
    bacc = chunk(n - nb)
    facc = None
    result = None
    for k in range(1, nb + 1):
        if nf > 0 and k == nb - nf + 1:
            facc = chunk(nf)
        recv_b = _from_wire(_send(_to_wire(bacc), bwd))
        recv_f = _from_wire(_send(_to_wire(facc), fwd)) if facc is not None else None
        if k < nb:
            bacc = _combine(recv_b, chunk((k - nb) % n))
            if recv_f is not None:
                facc = _combine(recv_f, chunk(nb - k))
        else:
            result = _combine(chunk(0), recv_b)
            if recv_f is not None:
                result = _combine(result, recv_f)
    return result


def _local(nz, nx, states, norm_gain, key_weight, value_weight, pass_len, retrieval, queries):
    blocks, tokens, model_width = states.shape
    inner = key_weight.shape[1]
    heads = inner // HS
    rows_here = key_weight.shape[0]
    n_dp = nz * nx
    dpi = lax.axis_index("dp")
    zi = dpi // nx
    xi = dpi % nx
    xf = _ring_perm(nz, nx, "x", 1)
    xb = _ring_perm(nz, nx, "x", -1)
    zf = _ring_perm(nz, nx, "z", 1)
    zb = _ring_perm(nz, nx, "z", -1)
    wkv = jnp.concatenate([key_weight, value_weight], axis=1)
    wx = _gather_ring(wkv, nx, xf, xb)
    wzx = _gather_ring(wx, nz, zf, zb)
    q_all = lax.all_gather(queries, "dp", axis=0, tiled=True)
    widened = states.astype(jnp.float32)
    mean_square = jnp.mean(widened * widened, axis=-1, keepdims=True)
    normed = (widened * lax.rsqrt(mean_square + 1e-06) * norm_gain).astype(jnp.bfloat16)
    flat = normed.reshape(blocks * tokens, nz, nx, rows_here)
    flat = jnp.roll(flat, -zi, axis=1)
    flat = jnp.roll(flat, -xi, axis=2)
    kv = jnp.dot(
        flat.reshape(blocks * tokens, model_width),
        wzx.reshape(model_width, 2 * inner),
        preferred_element_type=jnp.float32,
    ).astype(jnp.bfloat16)
    keys = kv[:, :inner].reshape(blocks, tokens, heads, HS)
    values = kv[:, inner:].reshape(blocks, tokens, heads, HS)
    n_q, answer_len, _ = q_all.shape
    q_heads = q_all.reshape(n_q, answer_len, heads, HS)
    scores = jnp.einsum("qthe,pshe->qhtps", q_heads, keys, preferred_element_type=jnp.float32)
    local_ids = retrieval - dpi * blocks
    owned = (local_ids >= 0) & (local_ids < blocks)
    onehot = (local_ids[:, None, :] == jnp.arange(blocks, dtype=jnp.int32)[None, :, None]) & owned[
        :, None, :
    ]
    picked = jnp.any(onehot, axis=2)
    positions = jnp.arange(tokens, dtype=jnp.int32)
    live = picked[:, :, None] & (positions[None, None, :] < pass_len[None, :, None])
    live5 = live[:, None, None, :, :]
    masked = jnp.where(live5, scores, -jnp.inf)
    m_loc = jnp.max(masked, axis=(3, 4))
    e = jnp.where(live5, jnp.exp(scores - m_loc[..., None, None]), 0.0)
    l_loc = jnp.sum(e, axis=(3, 4))
    e_pass = jnp.sum(e, axis=4)
    e_slot = jnp.einsum(
        "qhtp,qpj->qhtj", e_pass, onehot.astype(jnp.float32), precision=lax.Precision.HIGHEST
    )
    o_loc = jnp.einsum(
        "qhtps,pshe->qthe", e, values.astype(jnp.float32), precision=lax.Precision.HIGHEST
    )
    n_local_q = n_q // n_dp

    def split_q(a):
        return a.reshape((nz, nx, n_local_q) + a.shape[1:])

    state = jax.tree.map(split_q, (m_loc, l_loc, o_loc, e_slot))
    state = _reduce_ring(state, 1, xi, nx, xf, xb)
    state = _reduce_ring(state, 0, zi, nz, zf, zb)
    m_fin, l_fin, o_fin, e_fin = state
    context = o_fin / jnp.swapaxes(l_fin, -1, -2)[..., None]
    context = context.reshape(n_local_q, answer_len, inner).astype(jnp.bfloat16)
    mass = jnp.sum(e_fin / l_fin[..., None], axis=(1, 2)) / answer_len
    mass = lax.psum(mass, ("section", "mp"))
    return (context, mass)


def solution(mesh):
    nz, nx = _plane_shape(mesh)
    in_specs = (
        P("dp", None, None),
        P(),
        P("dp", ("section", "mp")),
        P("dp", ("section", "mp")),
        P("dp"),
        P(),
        P("dp", None, ("section", "mp")),
    )
    out_specs = (P("dp", None, ("section", "mp")), P("dp", None))

    def body(*args):
        return _local(nz, nx, *args)

    return jax.shard_map(body, mesh=mesh, in_specs=in_specs, out_specs=out_specs, check_vma=False)
```

profile of v0, /device:TPU:1, one launch (start us, length us, event | category | flops | bytes accessed | tf_op | source)
XLA Modules:
  0.0 677.8 jit_solution(13137495287411351185)
XLA Ops:
  25.1 11.3 %collective-permute-start.4 = (bf16[4,64,1024]{2,1,0:T(8,128)(2,1)S(1)}, bf16[4,64,1024]{2,1,0:T(8,128)(2,1)S(1)}, u32[]{:S(2)}, u32[]{:S(2)}) collective-permute-start(bf16[4,64,1024]{2,1,0:T(8,128)(2,1)S(1)} %pad_maximum_fusion), channel_id=1, source_target_pairs={{0,240},{4,244},{8,248},{12,252},{16,0},{20,4},{24,8},{28,12},{32,... | collective-permute-start | bytes 1572872 | tf_op jit(solution)/shard_map/ppermute | solution.py:45
  38.3 6.7 collective-permute-done.4
  45.0 5.3 collective-permute-start.5
  52.3 5.8 collective-permute-done.5
  58.0 5.4 collective-permute-start.6
  70.7 5.3 collective-permute-start.7
  83.9 4.7 copy.71
  102.7 5.1 collective-permute-start.9
  114.8 4.9 collective-permute-start.10
  125.3 8.0 %collective-permute-done.17 = bf16[4,64,1024]{2,1,0:T(8,128)(2,1)S(1)} collective-permute-done((bf16[4,64,1024]{2,1,0:T(8,128)(2,1)S(1)}, bf16[4,64,1024]{2,1,0:T(8,128)(2,1)S(1)}, u32[]{:S(2)}, u32[]{:S(2)}) %collective-permute-start.17) | collective-permute-done | bytes 524320 | tf_op jit(solution)/shard_map/ppermute | solution.py:44
  139.9 4.8 collective-permute-done.18
  151.7 46.2 %all-gather.2.cloned.1.call-done = bf16[64,32,512]{2,1,0:T(8,128)(2,1)} async-done(((bf16[1,32,512]{2,1,0:T(8,128)(2,1)}), bf16[64,32,512]{2,1,0:T(8,128)(2,1)}) %all-gather.2.cloned.1.call-update) | async-done | bytes 2097168 | tf_op jit(solution)/shard_map/all_gather | solution.py:129
  197.8 6.7 reshape.804
  204.5 20.0 %fusion = (f32[64,8,32]{0,2,1:T(8,128)S(1)}, f32[8,8,24,64,32]{3,2,4,1,0:T(8,128)}) fusion(pred[64,8,24]{0,2,1:T(8,128)(4,1)S(1)} %broadcast_and_fusion, bf16[64,32,8,64,1]{3,2,1,0,4:T(8,128)(2,1)} %bitcast.753, bf16[8,24,8,64,1]{3,2,1,0,4:T(8,128)(2,1)S(1)} %bitcast.760), kind=kOutput, calls=%fused_computation.2 | convolution fusion | flops 408928256 | bytes 14954496 | tf_op jit(solution)/shard_map/qthe,pshe->qhtps/dot_general | solution.py:145
  224.7 22.8 %fusion.243 = (f32[64,8,32,8]{0,2,3,1:T(8,128)S(1)}, f32[64,8,32]{0,2,1:T(8,128)S(1)}, f32[64,8,32,8,24]{0,4,2,3,1:T(8,128)}) fusion(f32[64,8,32]{0,2,1:T(8,128)S(1)} %get-tuple-element.164, f32[8,8,24,64,32]{3,2,4,1,0:T(8,128)} %get-tuple-element.165, pred[64,8,24]{0,2,1:T(8,128)(4,1)S(1)} %broadcast_and_fusion), kind=kLoop, calls=%fused_computation.390 | loop fusion | flops 12435456 | bytes 25833472 | tf_op jit(solution)/shard_map/reduce_sum | solution.py:159
  270.2 4.8 collective-permute-start.27
  276.4 5.0 collective-permute-start.28
  282.8 4.8 collective-permute-start.29
  296.1 4.8 collective-permute-start.31
  333.7 7.5 %fusion.43 = f32[64,8,32,64]{3,2,1,0:T(8,128)S(1)} fusion(f32[64,8,32,8]{2,3,1,0:T(8,128)S(1)} %copy.118, s32[64,64]{1,0:T(8,128)} %copy-done.22, pred[64,64]{1,0:T(8,128)(4,1)S(1)} %get-tuple-element.71), kind=kOutput, calls=%fused_computation.70 | convolution fusion | flops 100728832 | bytes 4739072 | tf_op jit(solution)/shard_map/qhtp,qpj->qhtj/dot_general | solution.py:160
  362.7 16.9 %fusion.7 = f32[64,32,8,64]{0,3,1,2:T(8,128)} fusion(f32[64,8,32,8,24]{0,4,2,3,1:T(8,128)} %get-tuple-element.70, bf16[8,24,8,64,1]{3,2,1,0,4:T(8,128)(2,1)S(1)} %bitcast.759), kind=kOutput, calls=%fused_computation.15 | convolution fusion | flops 2415919104 | bytes 16973824 | tf_op jit(solution)/shard_map/qhtps,pshe->qthe/dot_general | solution.py:163
  379.6 9.8 %copy.78 = f32[64,32,8,64]{3,2,1,0:T(8,128)} copy(f32[64,32,8,64]{0,3,1,2:T(8,128)} %fusion.7) | data formatting | bytes 8388608 | tf_op jit(solution)/shard_map/qhtps,pshe->qthe/transpose | solution.py:163
  520.1 4.7 collective-permute-start.34
  618.6 51.0 %psum.7 = f32[1,64]{1,0:T(1,128)} all-reduce(f32[1,64]{1,0:T(1,128)S(1)} %multiply_bitcast_fusion), channel_id=1, replica_groups=mesh['section'=2,'dp'=64,'mp'=4] {'section','mp'}, use_global_device_ids=true, to_apply=%region_6.7 | all-reduce | flops 64 | bytes 512 | tf_op jit(solution)/shard_map/psum | solution.py:178
  (529 shorter events, 387.6 us)
Async XLA Ops:
  7.2 190.7 %all-gather.2.cloned.1.call-start = ((), (), s32[]{:S(2)}) async-start(), calls=%async_computation | async-start | bytes 2129920 | tf_op jit(solution)/shard_map/all_gather | solution.py:129
  25.1 19.9 %collective-permute-start.4 = (bf16[4,64,1024]{2,1,0:T(8,128)(2,1)S(1)}, bf16[4,64,1024]{2,1,0:T(8,128)(2,1)S(1)}, u32[]{:S(2)}, u32[]{:S(2)}) collective-permute-start(bf16[4,64,1024]{2,1,0:T(8,128)(2,1)S(1)} %pad_maximum_fusion), channel_id=1, source_target_pairs={{0,240},{4,244},{8,248},{12,252},{16,0},{20,4},{24,8},{28,12},{32,... | collective-permute-start | bytes 1572872 | tf_op jit(solution)/shard_map/ppermute | solution.py:45
  70.7 20.6 %collective-permute-start.7 = (bf16[4,64,1024]{2,1,0:T(8,128)(2,1)}, bf16[4,64,1024]{2,1,0:T(8,128)(2,1)}, u32[]{:S(2)}, u32[]{:S(2)}) collective-permute-start(bf16[4,64,1024]{2,1,0:T(8,128)(2,1)} %collective-permute-done.6), channel_id=1, source_target_pairs={{0,240},{4,244},{8,248},{12,252},{16,0},{20,4},{24,8},{28,12},{32,... | collective-permute-start | bytes 1572872 | tf_op jit(solution)/shard_map/ppermute | solution.py:45
  76.0 19.9 %collective-permute-start.14 = (bf16[4,64,1024]{2,1,0:T(8,128)(2,1)}, bf16[4,64,1024]{2,1,0:T(8,128)(2,1)}, u32[]{:S(2)}, u32[]{:S(2)}) collective-permute-start(bf16[4,64,1024]{2,1,0:T(8,128)(2,1)} %collective-permute-done.13), channel_id=1, source_target_pairs={{0,16},{4,20},{8,24},{12,28},{16,32},{20,36},{24,40},{28,44},{32,4... | collective-permute-start | bytes 1572872 | tf_op jit(solution)/shard_map/ppermute | solution.py:44
  114.8 20.4 %collective-permute-start.10 = (bf16[4,64,1024]{2,1,0:T(8,128)(2,1)S(1)}, bf16[4,64,1024]{2,1,0:T(8,128)(2,1)S(1)}, u32[]{:S(2)}, u32[]{:S(2)}) collective-permute-start(bf16[4,64,1024]{2,1,0:T(8,128)(2,1)S(1)} %collective-permute-done.9), channel_id=1, source_target_pairs={{0,240},{4,244},{8,248},{12,252},{16,0},{20,4},{24,8},{28,12},{32,... | collective-permute-start | bytes 1572872 | tf_op jit(solution)/shard_map/ppermute | solution.py:45
  322.4 21.0 %collective-permute-start.33 = (f32[1,8,32]{2,1,0:T(8,128)S(1)}, f32[1,8,32]{2,1,0:T(8,128)S(1)}, u32[]{:S(2)}, u32[]{:S(2)}) collective-permute-start(f32[1,8,32]{2,1,0:T(8,128)S(1)} %get-tuple-element.7), channel_id=1, source_target_pairs={{0,240},{4,244},{8,248},{12,252},{16,0},{20,4},{24,8},{28,12},{32,... | collective-permute-start | bytes 3080 | tf_op jit(solution)/shard_map/ppermute | solution.py:33
  325.5 17.9 %collective-permute-start.45 = (f32[1,8,32]{2,1,0:T(8,128)S(1)}, f32[1,8,32]{2,1,0:T(8,128)S(1)}, u32[]{:S(2)}, u32[]{:S(2)}) collective-permute-start(f32[1,8,32]{2,1,0:T(8,128)S(1)} %get-tuple-element.133), channel_id=1, source_target_pairs={{0,16},{4,20},{8,24},{12,28},{16,32},{20,36},{24,40},{28,44},{32,4... | collective-permute-start | bytes 3080 | tf_op jit(solution)/shard_map/ppermute | solution.py:33
  350.3 126.9 %collective-permute-start.74 = (bf16[16,1,8,32,64]{4,3,2,0,1:T(8,128)(2,1)}, bf16[16,1,8,32,64]{4,3,2,0,1:T(8,128)(2,1)S(1)}, u32[]{:S(2)}, u32[]{:S(2)}) collective-permute-start(bf16[16,1,8,32,64]{4,3,2,0,1:T(8,128)(2,1)} %get-tuple-element.73), channel_id=1, source_target_pairs={{0,12},{4,0},{8,4},{12,8},{16,28},{20,16},{24,20},{28,24},{32,44},... | collective-permute-start | bytes 1572872 | tf_op jit(solution)/shard_map/ppermute | solution.py:33
  352.2 149.5 %collective-permute-start.76 = (bf16[16,1,8,32,64]{4,3,2,0,1:T(8,128)(2,1)S(1)}, bf16[16,1,8,32,64]{4,3,2,0,1:T(8,128)(2,1)}, u32[]{:S(2)}, u32[]{:S(2)}) collective-permute-start(bf16[16,1,8,32,64]{4,3,2,0,1:T(8,128)(2,1)S(1)} %get-tuple-element.74), channel_id=1, source_target_pairs={{0,4},{4,8},{8,12},{12,0},{16,20},{20,24},{24,28},{28,16},{32,36},... | collective-permute-start | bytes 1572872 | tf_op jit(solution)/shard_map/ppermute | solution.py:33
  357.2 32.2 %collective-permute-start.61 = (f32[1,8,32]{2,1,0:T(8,128)S(1)}, f32[1,8,32]{2,1,0:T(8,128)S(1)}, u32[]{:S(2)}, u32[]{:S(2)}) collective-permute-start(f32[1,8,32]{2,1,0:T(8,128)S(1)} %get-tuple-element.50), channel_id=1, source_target_pairs={{0,240},{4,244},{8,248},{12,252},{16,0},{20,4},{24,8},{28,12},{32,... | collective-permute-start | bytes 3080 | tf_op jit(solution)/shard_map/ppermute | solution.py:33
  359.1 30.3 %collective-permute-start.68 = (f32[1,8,32]{2,1,0:T(8,128)S(1)}, f32[1,8,32]{2,1,0:T(8,128)S(1)}, u32[]{:S(2)}, u32[]{:S(2)}) collective-permute-start(f32[1,8,32]{2,1,0:T(8,128)S(1)} %get-tuple-element.126), channel_id=1, source_target_pairs={{0,16},{4,20},{8,24},{12,28},{16,32},{20,36},{24,40},{28,44},{32,4... | collective-permute-start | bytes 3080 | tf_op jit(solution)/shard_map/ppermute | solution.py:33
  390.8 20.0 %collective-permute-start.62 = (f32[1,8,32]{2,1,0:T(8,128)}, f32[1,8,32]{2,1,0:T(8,128)S(1)}, u32[]{:S(2)}, u32[]{:S(2)}) collective-permute-start(f32[1,8,32]{2,1,0:T(8,128)} %get-tuple-element.48), channel_id=1, source_target_pairs={{0,240},{4,244},{8,248},{12,252},{16,0},{20,4},{24,8},{28,12},{32,... | collective-permute-start | bytes 3080 | tf_op jit(solution)/shard_map/ppermute | solution.py:33
  393.9 17.5 %collective-permute-start.69 = (f32[1,8,32]{2,1,0:T(8,128)}, f32[1,8,32]{2,1,0:T(8,128)}, u32[]{:S(2)}, u32[]{:S(2)}) collective-permute-start(f32[1,8,32]{2,1,0:T(8,128)} %get-tuple-element.124), channel_id=1, source_target_pairs={{0,16},{4,20},{8,24},{12,28},{16,32},{20,36},{24,40},{28,44},{32,4... | collective-permute-start | bytes 3080 | tf_op jit(solution)/shard_map/ppermute | solution.py:33
  408.2 19.8 %collective-permute-start.46 = (f32[1,8,32]{2,1,0:T(8,128)}, f32[1,8,32]{2,1,0:T(8,128)}, u32[]{:S(2)}, u32[]{:S(2)}) collective-permute-start(f32[1,8,32]{2,1,0:T(8,128)} %get-tuple-element.131), channel_id=1, source_target_pairs={{0,16},{4,20},{8,24},{12,28},{16,32},{20,36},{24,40},{28,44},{32,4... | collective-permute-start | bytes 3080 | tf_op jit(solution)/shard_map/ppermute | solution.py:33
  431.3 17.1 %collective-permute-start.64 = (f32[1,8,32]{2,1,0:T(8,128)}, f32[1,8,32]{2,1,0:T(8,128)}, u32[]{:S(2)}, u32[]{:S(2)}) collective-permute-start(f32[1,8,32]{2,1,0:T(8,128)} %get-tuple-element.44), channel_id=1, source_target_pairs={{0,240},{4,244},{8,248},{12,252},{16,0},{20,4},{24,8},{28,12},{32,... | collective-permute-start | bytes 3080 | tf_op jit(solution)/shard_map/ppermute | solution.py:33
  445.3 51.9 %collective-permute-start.22 = (bf16[16,1,32,8,64]{4,3,2,0,1:T(8,128)(2,1)}, bf16[16,1,32,8,64]{4,3,2,0,1:T(8,128)(2,1)}, u32[]{:S(2)}, u32[]{:S(2)}) collective-permute-start(bf16[16,1,32,8,64]{4,3,2,0,1:T(8,128)(2,1)} %get-tuple-element.75), channel_id=1, source_target_pairs={{0,12},{4,0},{8,4},{12,8},{16,28},{20,16},{24,20},{28,24},{32,44},... | collective-permute-start | bytes 1572872 | tf_op jit(solution)/shard_map/ppermute | solution.py:33
  464.4 17.9 %collective-permute-start.48 = (f32[1,8,32]{2,1,0:T(8,128)}, f32[1,8,32]{2,1,0:T(8,128)}, u32[]{:S(2)}, u32[]{:S(2)}) collective-permute-start(f32[1,8,32]{2,1,0:T(8,128)} %get-tuple-element.135), channel_id=1, source_target_pairs={{0,16},{4,20},{8,24},{12,28},{16,32},{20,36},{24,40},{28,44},{32,4... | collective-permute-start | bytes 3080 | tf_op jit(solution)/shard_map/ppermute | solution.py:33
  467.7 16.9 %collective-permute-start.66 = (f32[1,8,32]{2,1,0:T(8,128)}, f32[1,8,32]{2,1,0:T(8,128)}, u32[]{:S(2)}, u32[]{:S(2)}) collective-permute-start(f32[1,8,32]{2,1,0:T(8,128)} %get-tuple-element.40), channel_id=1, source_target_pairs={{0,240},{4,244},{8,248},{12,252},{16,0},{20,4},{24,8},{28,12},{32,... | collective-permute-start | bytes 3080 | tf_op jit(solution)/shard_map/ppermute | solution.py:33
  482.4 30.6 %collective-permute-start.25 = (bf16[16,1,32,8,64]{4,3,2,0,1:T(8,128)(2,1)S(1)}, bf16[16,1,32,8,64]{4,3,2,0,1:T(8,128)(2,1)}, u32[]{:S(2)}, u32[]{:S(2)}) collective-permute-start(bf16[16,1,32,8,64]{4,3,2,0,1:T(8,128)(2,1)S(1)} %get-tuple-element.76), channel_id=1, source_target_pairs={{0,4},{4,8},{8,12},{12,0},{16,20},{20,24},{24,28},{28,16},{32,36},... | collective-permute-start | bytes 1572872 | tf_op jit(solution)/shard_map/ppermute | solution.py:33
  484.7 17.1 %collective-permute-start.75 = (bf16[16,1,8,32,64]{4,3,2,0,1:T(8,128)(2,1)}, bf16[16,1,8,32,64]{4,3,2,0,1:T(8,128)(2,1)S(1)}, u32[]{:S(2)}, u32[]{:S(2)}) collective-permute-start(bf16[16,1,8,32,64]{4,3,2,0,1:T(8,128)(2,1)} %fusion.18), channel_id=1, source_target_pairs={{0,12},{4,0},{8,4},{12,8},{16,28},{20,16},{24,20},{28,24},{32,44},... | collective-permute-start | bytes 1572872 | tf_op jit(solution)/shard_map/ppermute | solution.py:33
  506.1 27.5 %collective-permute-start.85 = (bf16[1,8,32,64]{3,2,1,0:T(8,128)(2,1)S(1)}, bf16[1,8,32,64]{3,2,1,0:T(8,128)(2,1)S(1)}, u32[]{:S(2)}, u32[]{:S(2)}) collective-permute-start(bf16[1,8,32,64]{3,2,1,0:T(8,128)(2,1)S(1)} %fusion.112), channel_id=1, source_target_pairs={{0,16},{4,20},{8,24},{12,28},{16,32},{20,36},{24,40},{28,44},{32,4... | collective-permute-start | bytes 98312 | tf_op jit(solution)/shard_map/ppermute | solution.py:33
  508.5 18.3 %collective-permute-start.77 = (bf16[1,8,32,64]{3,2,1,0:T(8,128)(2,1)S(1)}, bf16[1,8,32,64]{3,2,1,0:T(8,128)(2,1)S(1)}, u32[]{:S(2)}, u32[]{:S(2)}) collective-permute-start(bf16[1,8,32,64]{3,2,1,0:T(8,128)(2,1)S(1)} %fusion.111), channel_id=1, source_target_pairs={{0,240},{4,244},{8,248},{12,252},{16,0},{20,4},{24,8},{28,12},{32,... | collective-permute-start | bytes 98312 | tf_op jit(solution)/shard_map/ppermute | solution.py:33
  611.7 57.9 %collective-permute-start.41 = (bf16[1,32,8,64]{3,2,1,0:T(8,128)(2,1)S(1)}, bf16[1,32,8,64]{3,2,1,0:T(8,128)(2,1)S(1)}, u32[]{:S(2)}, u32[]{:S(2)}) collective-permute-start(bf16[1,32,8,64]{3,2,1,0:T(8,128)(2,1)S(1)} %get-tuple-element.89), channel_id=1, source_target_pairs={{0,240},{4,244},{8,248},{12,252},{16,0},{20,4},{24,8},{28,12},{32,... | collective-permute-start | bytes 98312 | tf_op jit(solution)/shard_map/ppermute | solution.py:33
  616.3 53.3 %collective-permute-start.55 = (bf16[1,32,8,64]{3,2,1,0:T(8,128)(2,1)S(1)}, bf16[1,32,8,64]{3,2,1,0:T(8,128)(2,1)S(1)}, u32[]{:S(2)}, u32[]{:S(2)}) collective-permute-start(bf16[1,32,8,64]{3,2,1,0:T(8,128)(2,1)S(1)} %get-tuple-element.90), channel_id=1, source_target_pairs={{0,16},{4,20},{8,24},{12,28},{16,32},{20,36},{24,40},{28,44},{32,4... | collective-permute-start | bytes 98312 | tf_op jit(solution)/shard_map/ppermute | solution.py:33
  (184 other events, 5471.5 us)
Sparse Core Ops, SparseCore 0:
  65.6 132.2 all-gather.1
where the time goes:
time: 690 us; the launch traced here: 678 us
  starting transfers between devices  303 us (44%)
  waiting for transfers between devices  96.9 us (14%)
  local copies, waits for them, and re-layouts  91.3 us (13%)
  other arithmetic  70.6 us (10%)
  blocking collectives  51 us (7%)
  matrix products  46.9 us (7%)
  between operations  17.8 us (3%)
    ppermute x72, starting transfers between devices, _send(): return jax.tree.map(lambda a: lax.ppermute(a, 'dp', perm), tree)  228 us
    psum x1, blocking collectives, _local(): mass = lax.psum(mass, ('section', 'mp'))  51 us
    all_gather x1, waiting for transfers between devices, _local(): q_all = lax.all_gather(queries, 'dp', axis=0, tiled=True)  46.2 us
    ppermute x8, starting transfers between devices, _gather_ring(): g = lax.ppermute(g, 'dp', bwd)  45.1 us
    mul x36, local copies, waits for them, and re-layouts, _combine(): o = oa * sa_o + ob * sb_o  43.7 us
    ppermute x8, waiting for transfers between devices, _gather_ring(): g = lax.ppermute(g, 'dp', bwd)  23 us
    reduce_sum x1, other arithmetic, _local(): e_pass = jnp.sum(e, axis=4)  22.8 us
    dot_general x1, matrix products, _local(): jnp.einsum('qthe,pshe->qhtps', q_heads, keys, preferred_element_type=jnp....  20 us
  transfers between devices with their start and end apart: 93, of which 20 were waited for; matrix products, arithmetic and copies ran while one was open for 22% of the time, Pallas kernels for 0%

commit v1 on v0

--- a/solution.py
+++ b/solution.py
@@ -126,7 +126,9 @@
     wkv = jnp.concatenate([key_weight, value_weight], axis=1)
     wx = _gather_ring(wkv, nx, xf, xb)
     wzx = _gather_ring(wx, nz, zf, zb)
-    q_all = lax.all_gather(queries, "dp", axis=0, tiled=True)
+    q_all = jnp.concatenate(
+        lax.all_to_all(jnp.stack(lax.psum(1, "dp") * [queries], axis=0), "dp", 0, 0), 0
+    )
     widened = states.astype(jnp.float32)
     mean_square = jnp.mean(widened * widened, axis=-1, keepdims=True)
     normed = (widened * lax.rsqrt(mean_square + 1e-06) * norm_gain).astype(jnp.bfloat16)

time: 690 us -> 723 us (1.048)
  the two profiles are of different devices: /device:TPU:1 before, /device:TPU:97 now
where the time goes in v1:
time: 723 us; the launch traced here: 710 us
  starting transfers between devices  301 us (42%)
  waiting for transfers between devices  153 us (21%)
  local copies, waits for them, and re-layouts  91.4 us (13%)
  other arithmetic  67.3 us (9%)
  matrix products  46.8 us (6%)
  blocking collectives  46.3 us (6%)
    ppermute x72, starting transfers between devices, _send(): return jax.tree.map(lambda a: lax.ppermute(a, 'dp', perm), tree)  220 us
    ppermute x8, waiting for transfers between devices, _gather_ring(): g = lax.ppermute(g, 'dp', bwd)  116 us
    psum x1, blocking collectives, _local(): mass = lax.psum(mass, ('section', 'mp'))  46.3 us
    mul x36, local copies, waits for them, and re-layouts, _combine(): o = oa * sa_o + ob * sb_o  41.9 us
    ppermute x8, starting transfers between devices, _gather_ring(): f = lax.ppermute(f, 'dp', fwd)  35 us
    ppermute x72, waiting for transfers between devices, _send(): return jax.tree.map(lambda a: lax.ppermute(a, 'dp', perm), tree)  25.8 us
    reduce_sum x1, other arithmetic, _local(): e_pass = jnp.sum(e, axis=4)  22.8 us
    dot_general x1, matrix products, _local(): jnp.einsum('qthe,pshe->qhtps', q_heads, keys, preferred_element_type=jnp....  20 us
  transfers between devices with their start and end apart: 93, of which 19 were waited for; matrix products, arithmetic and copies ran while one was open for 21% of the time, Pallas kernels for 0%

profile of v1, /device:TPU:97, one launch (start us, length us, event | category | flops | bytes accessed | tf_op | source)
XLA Modules:
  0.0 710.3 jit_solution(11707269707214116594)
XLA Ops:
  19.7 4.8 collective-permute-start.11
  26.9 15.9 %all-to-all-start = ((bf16[64,1,32,512]{3,2,1,0:T(8,128)(2,1)}), bf16[64,1,32,512]{3,2,1,0:T(8,128)(2,1)}, u32[]{:S(2)}, u32[]{:S(2)}) async-start(bf16[64,1,32,512]{3,2,1,0:T(8,128)(2,1)} %stack.68), calls=%async_computation | async-start | bytes 4194304 | tf_op jit(solution)/shard_map/all_to_all | solution.py:130
  49.4 96.6 %collective-permute-done.5 = bf16[4,64,1024]{2,1,0:T(8,128)(2,1)S(1)} collective-permute-done((bf16[4,64,1024]{2,1,0:T(8,128)(2,1)S(1)}, bf16[4,64,1024]{2,1,0:T(8,128)(2,1)S(1)}, u32[]{:S(2)}, u32[]{:S(2)}) %collective-permute-start.5) | collective-permute-done | bytes 524320 | tf_op jit(solution)/shard_map/ppermute | solution.py:45
  147.9 4.6 collective-permute-start.13
  152.9 8.1 %collective-permute-done.6 = bf16[4,64,1024]{2,1,0:T(8,128)(2,1)} collective-permute-done((bf16[4,64,1024]{2,1,0:T(8,128)(2,1)S(1)}, bf16[4,64,1024]{2,1,0:T(8,128)(2,1)}, u32[]{:S(2)}, u32[]{:S(2)}) %collective-permute-start.6) | collective-permute-done | bytes 524320 | tf_op jit(solution)/shard_map/ppermute | solution.py:45
  162.9 4.6 collective-permute-start.14
  173.5 4.8 copy.71
  182.8 4.6 collective-permute-start.15
  188.8 5.8 collective-permute-done.8
  202.3 5.1 collective-permute-done.9
  220.1 5.4 collective-permute-start.18
  228.7 5.1 collective-permute-done.19
  240.1 6.7 reshape_reshape.3
  246.7 20.0 %fusion = (f32[64,8,32]{0,2,1:T(8,128)S(1)}, f32[8,8,24,64,32]{3,2,4,1,0:T(8,128)}) fusion(pred[64,8,24]{0,2,1:T(8,128)(4,1)S(1)} %broadcast_and_fusion, bf16[64,32,8,64,1]{3,2,1,0,4:T(8,128)(2,1)} %bitcast.756, bf16[8,24,8,64,1]{3,2,1,0,4:T(8,128)(2,1)S(1)} %bitcast.763), kind=kOutput, calls=%fused_computation.2 | convolution fusion | flops 408928256 | bytes 14954496 | tf_op jit(solution)/shard_map/qthe,pshe->qhtps/dot_general | solution.py:147
  266.9 22.8 %fusion.243 = (f32[64,8,32,8]{0,2,3,1:T(8,128)S(1)}, f32[64,8,32]{0,2,1:T(8,128)S(1)}, f32[64,8,32,8,24]{0,4,2,3,1:T(8,128)}) fusion(f32[64,8,32]{0,2,1:T(8,128)S(1)} %get-tuple-element.164, f32[8,8,24,64,32]{3,2,4,1,0:T(8,128)} %get-tuple-element.165, pred[64,8,24]{0,2,1:T(8,128)(4,1)S(1)} %broadcast_and_fusion), kind=kLoop, calls=%fused_computation.390 | loop fusion | flops 12435456 | bytes 25833472 | tf_op jit(solution)/shard_map/reduce_sum | solution.py:161
  349.6 5.0 collective-permute-start.44
  375.7 7.5 %fusion.43 = f32[64,8,32,64]{3,2,1,0:T(8,128)S(1)} fusion(f32[64,8,32,8]{2,3,1,0:T(8,128)S(1)} %copy.118, s32[64,64]{1,0:T(8,128)} %copy-done.21, pred[64,64]{1,0:T(8,128)(4,1)S(1)} %get-tuple-element.71), kind=kOutput, calls=%fused_computation.70 | convolution fusion | flops 100728832 | bytes 4739072 | tf_op jit(solution)/shard_map/qhtp,qpj->qhtj/dot_general | solution.py:162
  383.3 4.7 collective-permute-start.67
  400.2 4.8 collective-permute-start.68
  405.0 16.9 %fusion.7 = f32[64,32,8,64]{0,3,1,2:T(8,128)} fusion(f32[64,8,32,8,24]{0,4,2,3,1:T(8,128)} %get-tuple-element.70, bf16[8,24,8,64,1]{3,2,1,0,4:T(8,128)(2,1)S(1)} %bitcast.762), kind=kOutput, calls=%fused_computation.15 | convolution fusion | flops 2415919104 | bytes 16973824 | tf_op jit(solution)/shard_map/qhtps,pshe->qthe/dot_general | solution.py:165
  421.8 9.8 %copy.78 = f32[64,32,8,64]{3,2,1,0:T(8,128)} copy(f32[64,32,8,64]{0,3,1,2:T(8,128)} %fusion.7) | data formatting | bytes 8388608 | tf_op jit(solution)/shard_map/qhtps,pshe->qthe/transpose | solution.py:165
  479.5 4.6 collective-permute-start.71
  616.2 4.8 collective-permute-start.52
  662.7 46.3 %psum.7 = f32[1,64]{1,0:T(1,128)} all-reduce(f32[1,64]{1,0:T(1,128)S(1)} %multiply_bitcast_fusion), channel_id=1, replica_groups=mesh['section'=2,'dp'=64,'mp'=4] {'section','mp'}, use_global_device_ids=true, to_apply=%region_6.7 | all-reduce | flops 64 | bytes 512 | tf_op jit(solution)/shard_map/psum | solution.py:180
  (525 shorter events, 387.1 us)
Async XLA Ops:
  17.7 25.1 %collective-permute-start.4 = (bf16[4,64,1024]{2,1,0:T(8,128)(2,1)S(1)}, bf16[4,64,1024]{2,1,0:T(8,128)(2,1)S(1)}, u32[]{:S(2)}, u32[]{:S(2)}) collective-permute-start(bf16[4,64,1024]{2,1,0:T(8,128)(2,1)S(1)} %pad_maximum_fusion), channel_id=1, source_target_pairs={{0,240},{4,244},{8,248},{12,252},{16,0},{20,4},{24,8},{28,12},{32,... | collective-permute-start | bytes 1572872 | tf_op jit(solution)/shard_map/ppermute | solution.py:45
  19.7 25.4 %collective-permute-start.11 = (bf16[4,64,1024]{2,1,0:T(8,128)(2,1)S(1)}, bf16[4,64,1024]{2,1,0:T(8,128)(2,1)S(1)}, u32[]{:S(2)}, u32[]{:S(2)}) collective-permute-start(bf16[4,64,1024]{2,1,0:T(8,128)(2,1)S(1)} %pad_maximum_fusion), channel_id=1, source_target_pairs={{0,16},{4,20},{8,24},{12,28},{16,32},{20,36},{24,40},{28,44},{32,4... | collective-permute-start | bytes 1572872 | tf_op jit(solution)/shard_map/ppermute | solution.py:44
  26.9 213.1 %all-to-all-start = ((bf16[64,1,32,512]{3,2,1,0:T(8,128)(2,1)}), bf16[64,1,32,512]{3,2,1,0:T(8,128)(2,1)}, u32[]{:S(2)}, u32[]{:S(2)}) async-start(bf16[64,1,32,512]{3,2,1,0:T(8,128)(2,1)} %stack.68), calls=%async_computation | async-start | bytes 4194304 | tf_op jit(solution)/shard_map/all_to_all | solution.py:130
  42.9 103.1 %collective-permute-start.5 = (bf16[4,64,1024]{2,1,0:T(8,128)(2,1)S(1)}, bf16[4,64,1024]{2,1,0:T(8,128)(2,1)S(1)}, u32[]{:S(2)}, u32[]{:S(2)}) collective-permute-start(bf16[4,64,1024]{2,1,0:T(8,128)(2,1)S(1)} %collective-permute-done.4), channel_id=1, source_target_pairs={{0,240},{4,244},{8,248},{12,252},{16,0},{20,4},{24,8},{28,12},{32,... | collective-permute-start | bytes 1572872 | tf_op jit(solution)/shard_map/ppermute | solution.py:45
  45.1 102.8 %collective-permute-start.12 = (bf16[4,64,1024]{2,1,0:T(8,128)(2,1)S(1)}, bf16[4,64,1024]{2,1,0:T(8,128)(2,1)S(1)}, u32[]{:S(2)}, u32[]{:S(2)}) collective-permute-start(bf16[4,64,1024]{2,1,0:T(8,128)(2,1)S(1)} %collective-permute-done.11), channel_id=1, source_target_pairs={{0,16},{4,20},{8,24},{12,28},{16,32},{20,36},{24,40},{28,44},{32,4... | collective-permute-start | bytes 1572872 | tf_op jit(solution)/shard_map/ppermute | solution.py:44
  161.0 19.8 %collective-permute-start.7 = (bf16[4,64,1024]{2,1,0:T(8,128)(2,1)}, bf16[4,64,1024]{2,1,0:T(8,128)(2,1)}, u32[]{:S(2)}, u32[]{:S(2)}) collective-permute-start(bf16[4,64,1024]{2,1,0:T(8,128)(2,1)} %collective-permute-done.6), channel_id=1, source_target_pairs={{0,240},{4,244},{8,248},{12,252},{16,0},{20,4},{24,8},{28,12},{32,... | collective-permute-start | bytes 1572872 | tf_op jit(solution)/shard_map/ppermute | solution.py:45
  162.9 19.9 %collective-permute-start.14 = (bf16[4,64,1024]{2,1,0:T(8,128)(2,1)}, bf16[4,64,1024]{2,1,0:T(8,128)(2,1)}, u32[]{:S(2)}, u32[]{:S(2)}) collective-permute-start(bf16[4,64,1024]{2,1,0:T(8,128)(2,1)} %collective-permute-done.13), channel_id=1, source_target_pairs={{0,16},{4,20},{8,24},{12,28},{16,32},{20,36},{24,40},{28,44},{32,4... | collective-permute-start | bytes 1572872 | tf_op jit(solution)/shard_map/ppermute | solution.py:44
  365.4 22.6 %collective-permute-start.33 = (f32[1,8,32]{2,1,0:T(8,128)S(1)}, f32[1,8,32]{2,1,0:T(8,128)S(1)}, u32[]{:S(2)}, u32[]{:S(2)}) collective-permute-start(f32[1,8,32]{2,1,0:T(8,128)S(1)} %get-tuple-element.7), channel_id=1, source_target_pairs={{0,240},{4,244},{8,248},{12,252},{16,0},{20,4},{24,8},{28,12},{32,... | collective-permute-start | bytes 3080 | tf_op jit(solution)/shard_map/ppermute | solution.py:33
  367.4 20.7 %collective-permute-start.45 = (f32[1,8,32]{2,1,0:T(8,128)S(1)}, f32[1,8,32]{2,1,0:T(8,128)S(1)}, u32[]{:S(2)}, u32[]{:S(2)}) collective-permute-start(f32[1,8,32]{2,1,0:T(8,128)S(1)} %get-tuple-element.133), channel_id=1, source_target_pairs={{0,16},{4,20},{8,24},{12,28},{16,32},{20,36},{24,40},{28,44},{32,4... | collective-permute-start | bytes 3080 | tf_op jit(solution)/shard_map/ppermute | solution.py:33
  392.3 129.9 %collective-permute-start.74 = (bf16[16,1,8,32,64]{4,3,2,0,1:T(8,128)(2,1)}, bf16[16,1,8,32,64]{4,3,2,0,1:T(8,128)(2,1)S(1)}, u32[]{:S(2)}, u32[]{:S(2)}) collective-permute-start(bf16[16,1,8,32,64]{4,3,2,0,1:T(8,128)(2,1)} %get-tuple-element.73), channel_id=1, source_target_pairs={{0,12},{4,0},{8,4},{12,8},{16,28},{20,16},{24,20},{28,24},{32,44},... | collective-permute-start | bytes 1572872 | tf_op jit(solution)/shard_map/ppermute | solution.py:33
  394.2 151.6 %collective-permute-start.76 = (bf16[16,1,8,32,64]{4,3,2,0,1:T(8,128)(2,1)S(1)}, bf16[16,1,8,32,64]{4,3,2,0,1:T(8,128)(2,1)}, u32[]{:S(2)}, u32[]{:S(2)}) collective-permute-start(bf16[16,1,8,32,64]{4,3,2,0,1:T(8,128)(2,1)S(1)} %get-tuple-element.74), channel_id=1, source_target_pairs={{0,4},{4,8},{8,12},{12,0},{16,20},{20,24},{24,28},{28,16},{32,36},... | collective-permute-start | bytes 1572872 | tf_op jit(solution)/shard_map/ppermute | solution.py:33
  398.3 33.4 %collective-permute-start.61 = (f32[1,8,32]{2,1,0:T(8,128)S(1)}, f32[1,8,32]{2,1,0:T(8,128)S(1)}, u32[]{:S(2)}, u32[]{:S(2)}) collective-permute-start(f32[1,8,32]{2,1,0:T(8,128)S(1)} %get-tuple-element.50), channel_id=1, source_target_pairs={{0,240},{4,244},{8,248},{12,252},{16,0},{20,4},{24,8},{28,12},{32,... | collective-permute-start | bytes 3080 | tf_op jit(solution)/shard_map/ppermute | solution.py:33
  400.2 31.5 %collective-permute-start.68 = (f32[1,8,32]{2,1,0:T(8,128)S(1)}, f32[1,8,32]{2,1,0:T(8,128)S(1)}, u32[]{:S(2)}, u32[]{:S(2)}) collective-permute-start(f32[1,8,32]{2,1,0:T(8,128)S(1)} %get-tuple-element.126), channel_id=1, source_target_pairs={{0,16},{4,20},{8,24},{12,28},{16,32},{20,36},{24,40},{28,44},{32,4... | collective-permute-start | bytes 3080 | tf_op jit(solution)/shard_map/ppermute | solution.py:33
  433.0 21.4 %collective-permute-start.62 = (f32[1,8,32]{2,1,0:T(8,128)}, f32[1,8,32]{2,1,0:T(8,128)S(1)}, u32[]{:S(2)}, u32[]{:S(2)}) collective-permute-start(f32[1,8,32]{2,1,0:T(8,128)} %get-tuple-element.48), channel_id=1, source_target_pairs={{0,240},{4,244},{8,248},{12,252},{16,0},{20,4},{24,8},{28,12},{32,... | collective-permute-start | bytes 3080 | tf_op jit(solution)/shard_map/ppermute | solution.py:33
  434.9 20.1 %collective-permute-start.69 = (f32[1,8,32]{2,1,0:T(8,128)}, f32[1,8,32]{2,1,0:T(8,128)}, u32[]{:S(2)}, u32[]{:S(2)}) collective-permute-start(f32[1,8,32]{2,1,0:T(8,128)} %get-tuple-element.124), channel_id=1, source_target_pairs={{0,16},{4,20},{8,24},{12,28},{16,32},{20,36},{24,40},{28,44},{32,4... | collective-permute-start | bytes 3080 | tf_op jit(solution)/shard_map/ppermute | solution.py:33
  451.6 20.1 %collective-permute-start.46 = (f32[1,8,32]{2,1,0:T(8,128)}, f32[1,8,32]{2,1,0:T(8,128)}, u32[]{:S(2)}, u32[]{:S(2)}) collective-permute-start(f32[1,8,32]{2,1,0:T(8,128)} %get-tuple-element.131), channel_id=1, source_target_pairs={{0,16},{4,20},{8,24},{12,28},{16,32},{20,36},{24,40},{28,44},{32,4... | collective-permute-start | bytes 3080 | tf_op jit(solution)/shard_map/ppermute | solution.py:33
  473.0 18.5 %collective-permute-start.47 = (f32[1,8,32]{2,1,0:T(8,128)}, f32[1,8,32]{2,1,0:T(8,128)S(1)}, u32[]{:S(2)}, u32[]{:S(2)}) collective-permute-start(f32[1,8,32]{2,1,0:T(8,128)} %get-tuple-element.139), channel_id=1, source_target_pairs={{0,16},{4,20},{8,24},{12,28},{16,32},{20,36},{24,40},{28,44},{32,4... | collective-permute-start | bytes 3080 | tf_op jit(solution)/shard_map/ppermute | solution.py:33
  491.5 49.7 %collective-permute-start.22 = (bf16[16,1,32,8,64]{4,3,2,0,1:T(8,128)(2,1)}, bf16[16,1,32,8,64]{4,3,2,0,1:T(8,128)(2,1)}, u32[]{:S(2)}, u32[]{:S(2)}) collective-permute-start(bf16[16,1,32,8,64]{4,3,2,0,1:T(8,128)(2,1)} %get-tuple-element.75), channel_id=1, source_target_pairs={{0,12},{4,0},{8,4},{12,8},{16,28},{20,16},{24,20},{28,24},{32,44},... | collective-permute-start | bytes 1572872 | tf_op jit(solution)/shard_map/ppermute | solution.py:33
  510.7 18.2 %collective-permute-start.48 = (f32[1,8,32]{2,1,0:T(8,128)}, f32[1,8,32]{2,1,0:T(8,128)}, u32[]{:S(2)}, u32[]{:S(2)}) collective-permute-start(f32[1,8,32]{2,1,0:T(8,128)} %get-tuple-element.135), channel_id=1, source_target_pairs={{0,16},{4,20},{8,24},{12,28},{16,32},{20,36},{24,40},{28,44},{32,4... | collective-permute-start | bytes 3080 | tf_op jit(solution)/shard_map/ppermute | solution.py:33
  528.8 28.7 %collective-permute-start.25 = (bf16[16,1,32,8,64]{4,3,2,0,1:T(8,128)(2,1)S(1)}, bf16[16,1,32,8,64]{4,3,2,0,1:T(8,128)(2,1)}, u32[]{:S(2)}, u32[]{:S(2)}) collective-permute-start(bf16[16,1,32,8,64]{4,3,2,0,1:T(8,128)(2,1)S(1)} %get-tuple-element.76), channel_id=1, source_target_pairs={{0,4},{4,8},{8,12},{12,0},{16,20},{20,24},{24,28},{28,16},{32,36},... | collective-permute-start | bytes 1572872 | tf_op jit(solution)/shard_map/ppermute | solution.py:33
  551.9 23.9 %collective-permute-start.85 = (bf16[1,8,32,64]{3,2,1,0:T(8,128)(2,1)S(1)}, bf16[1,8,32,64]{3,2,1,0:T(8,128)(2,1)S(1)}, u32[]{:S(2)}, u32[]{:S(2)}) collective-permute-start(bf16[1,8,32,64]{3,2,1,0:T(8,128)(2,1)S(1)} %fusion.112), channel_id=1, source_target_pairs={{0,16},{4,20},{8,24},{12,28},{16,32},{20,36},{24,40},{28,44},{32,4... | collective-permute-start | bytes 98312 | tf_op jit(solution)/shard_map/ppermute | solution.py:33
  567.3 18.2 %collective-permute-start.49 = (bf16[1,32,8,64]{3,2,1,0:T(8,128)(2,1)S(1)}, bf16[1,32,8,64]{3,2,1,0:T(8,128)(2,1)S(1)}, u32[]{:S(2)}, u32[]{:S(2)}) collective-permute-start(bf16[1,32,8,64]{3,2,1,0:T(8,128)(2,1)S(1)} %get-tuple-element.102), channel_id=1, source_target_pairs={{0,16},{4,20},{8,24},{12,28},{16,32},{20,36},{24,40},{28,44},{32,4... | collective-permute-start | bytes 98312 | tf_op jit(solution)/shard_map/ppermute | solution.py:33
  655.9 53.1 %collective-permute-start.41 = (bf16[1,32,8,64]{3,2,1,0:T(8,128)(2,1)S(1)}, bf16[1,32,8,64]{3,2,1,0:T(8,128)(2,1)S(1)}, u32[]{:S(2)}, u32[]{:S(2)}) collective-permute-start(bf16[1,32,8,64]{3,2,1,0:T(8,128)(2,1)S(1)} %get-tuple-element.89), channel_id=1, source_target_pairs={{0,240},{4,244},{8,248},{12,252},{16,0},{20,4},{24,8},{28,12},{32,... | collective-permute-start | bytes 98312 | tf_op jit(solution)/shard_map/ppermute | solution.py:33
  657.8 51.2 %collective-permute-start.55 = (bf16[1,32,8,64]{3,2,1,0:T(8,128)(2,1)S(1)}, bf16[1,32,8,64]{3,2,1,0:T(8,128)(2,1)S(1)}, u32[]{:S(2)}, u32[]{:S(2)}) collective-permute-start(bf16[1,32,8,64]{3,2,1,0:T(8,128)(2,1)S(1)} %get-tuple-element.90), channel_id=1, source_target_pairs={{0,16},{4,20},{8,24},{12,28},{16,32},{20,36},{24,40},{28,44},{32,4... | collective-permute-start | bytes 98312 | tf_op jit(solution)/shard_map/ppermute | solution.py:33
  (182 other events, 5252.0 us)
